TPU v7x, 32 devices: a whole 2x2x4 slice. The times are simulated.
32 devices in a mesh: cell: 16 (over z, y, core), bin: 2 (over x).
Axes of the slice: x: 2, y: 2, z: 4, core: 2. Of those that a mesh axis runs over, the one named last changes fastest.
Arguments:
- tensor: float32 [96, 4096, 1024], P('cell', None, 'bin'), may hold values from -6 to 6
- cell_factor: float32 [4096, 128], P('cell'), may hold values from -4 to 4
- bin_factor: float32 [1024, 128], P('bin'), may hold values from -4 to 4
Outputs:
- updated: float32 [96, 128], P('cell', 'bin')
All inputs are finite; a program needn't handle non-finite values.
Results may differ from a plain program's by a relative error of at most 0.000096.
Values sent between devices are 32-bit elements; how exact they have to be, the bound alone decides.
No kernel may reach another device: no remote copies, remote signals or barrier semaphores. Data moves between devices by JAX's collectives and lax.ppermute only.
A program may use at most 128 MiB of HBM per device.

v0:
```python
import jax
import jax.numpy as jnp
from jax import lax
from jax.sharding import PartitionSpec as P


def body(tensor, cell_factor, bin_factor):
    highest = lax.Precision.HIGHEST
    image_rows, cell_count, bin_count = tensor.shape
    rank_cols = bin_factor.shape[1]
    projected = jnp.dot(
        tensor.reshape(image_rows * cell_count, bin_count), bin_factor, precision=highest
    )
    projected = projected.reshape(image_rows, cell_count, rank_cols)
    bin_local = jnp.dot(bin_factor.T, bin_factor, precision=highest)
    gram_bin = lax.psum(bin_local, "bin")
    mttkrp = jnp.sum(
        projected * lax.all_gather(cell_factor, "cell", axis=0, tiled=True)[None, :, :], axis=1
    )
    cell_local = jnp.dot(cell_factor.T, cell_factor, precision=highest)
    gram_cell = lax.psum(cell_local, "cell")
    gram = gram_cell * gram_bin
    chol_lower = jnp.linalg.cholesky(gram)
    totals = lax.psum(mttkrp, "bin")
    solved = jax.scipy.linalg.cho_solve((chol_lower, True), totals.T).T
    own_cols = rank_cols // lax.axis_size("bin")
    updated = lax.dynamic_slice_in_dim(solved, lax.axis_index("bin") * own_cols, own_cols, 1)
    return updated


def solution(mesh):
    placed = (P("cell", None, "bin"), P("cell", None), P("bin", None))
    return jax.shard_map(
        body, mesh=mesh, in_specs=placed, out_specs=P("cell", "bin"), check_vma=False
    )
```

profile of v0, /device:TPU:0, one launch (start us, length us, event | category | flops | bytes accessed | tf_op | source)
XLA Modules:
  0.0 223.3 jit_solution(393272512199881900)
XLA Ops:
  6.5 0.0 copy-start
  6.5 0.0 all-reduce.3.cloned.1.call-start
  6.5 2.0 fusion.7
  8.6 0.0 all-reduce.3.cloned.1.call-update
  8.6 0.0 all-reduce.5.cloned.1.call-start
  8.6 0.0 copy-done
  8.6 1.2 fusion.8
  9.8 0.0 all-reduce.5.cloned.1.call-update
  9.9 0.0 all-gather.2.cloned.1.call-start
  9.9 0.7 all-gather.2.cloned.1.call-update
  10.6 87.4 %all-reduce.3.cloned.1.call-done = f32[128,128]{0,1:T(8,128)} async-done(((f32[128,128]{0,1:T(8,128)}), f32[128,128]{0,1:T(8,128)}) %all-reduce.3.cloned.1.call-update) | async-done | bytes 65552 | tf_op jit(solution)/shard_map/psum | solution.py:21
  98.0 24.7 %all-reduce.5.cloned.1.call-done = f32[128,128]{0,1:T(8,128)} async-done(((f32[128,128]{0,1:T(8,128)}), f32[128,128]{0,1:T(8,128)}) %all-reduce.5.cloned.1.call-update) | async-done | bytes 65552 | tf_op jit(solution)/shard_map/psum | solution.py:16
  122.7 0.9 mul.14
  123.6 0.1 copy.9
  123.7 11.7 %cholesky.16 = f32[128,128]{1,0:T(8,128)S(1)} custom-call(f32[128,128]{1,0:T(8,128)S(1)} %fusion.6), custom_call_target="Cholesky" | custom-call | tf_op jit(solution)/shard_map/jit(cholesky)/cholesky | solution.py:23
  135.5 0.6 compare_reduce_fusion
  136.1 0.7 fusion.1
  136.8 9.8 %custom-call.10 = f32[1,128,128]{1,2,0:T(8,128)S(1)} custom-call(f32[1,128,128]{2,1,0:T(8,128)S(1)} %fusion.1), custom_call_target="InvertDiagBlocksLowerTriangular" | custom-call | tf_op jit(solution)/shard_map/jit(_cho_solve)/triangular_solve | solution.py:25
  146.6 20.2 %all-gather.2.cloned.1.call-done = f32[4096,128]{1,0:T(8,128)} async-done(((f32[256,128]{1,0:T(8,128)}), f32[4096,128]{1,0:T(8,128)}) %all-gather.2.cloned.1.call-update) | async-done | bytes 2097168 | tf_op jit(solution)/shard_map/all_gather | solution.py:18
  166.8 43.8 %multiply_reduce_fusion = f32[6,128]{1,0:T(8,128)S(1)} fusion(f32[6,4096,512]{2,1,0:T(8,128)} %param.3, f32[4096,128]{1,0:T(8,128)} %all-gather.2.cloned.1.call-done, f32[512,128]{1,0:T(8,128)S(1)} %copy-done), kind=kOutput, calls=%fused_computation | convolution fusion | flops 19333644288 | bytes 52694016 | tf_op jit(solution)/shard_map/dot_general | solution.py:11
  210.7 4.9 %psum.23 = f32[6,128]{1,0:T(8,128)S(1)} all-reduce(f32[6,128]{1,0:T(8,128)S(1)} %multiply_reduce_fusion), channel_id=1, replica_groups=mesh['cell'=16,'bin'=2] {'bin'}, use_global_device_ids=true, to_apply=%region_5.6 | all-reduce | flops 768 | bytes 6144 | tf_op jit(solution)/shard_map/psum | solution.py:24
  215.6 0.3 fusion.4
  215.9 0.2 fusion.2
  216.1 0.7 constant_dynamic-slice_fusion
  (2 shorter events, 0.0 us)
Async XLA Ops:
  6.5 2.1 copy-start
  6.5 91.5 %all-reduce.3.cloned.1.call-start = ((), (), s32[]{:S(2)}) async-start(), calls=%async_computation | async-start | bytes 131072 | tf_op jit(solution)/shard_map/psum | solution.py:21
  8.6 114.1 %all-reduce.5.cloned.1.call-start = ((), (), s32[]{:S(2)}) async-start(), calls=%async_computation.1 | async-start | bytes 131072 | tf_op jit(solution)/shard_map/psum | solution.py:16
  9.9 156.9 %all-gather.2.cloned.1.call-start = ((), (), s32[]{:S(2)}) async-start(), calls=%async_computation.2 | async-start | bytes 2228224 | tf_op jit(solution)/shard_map/all_gather | solution.py:18
Sparse Core Ops, SparseCore 0:
  10.8 87.1 all-reduce.2
  100.3 22.3 all-reduce.4
  125.1 41.6 all-gather.1
where the time goes:
time: 224 us; the launch traced here: 223 us
  waiting for transfers between devices  133 us (59%)
  matrix products  47.5 us (21%)
  other arithmetic  23.8 us (11%)
  between operations  13.2 us (6%)
  blocking collectives  4.95 us (2%)
    psum x1, waiting for transfers between devices, body(): gram_cell = lax.psum(cell_local, 'cell')  87.4 us
    dot_general x1, matrix products, body(): jnp.dot(tensor.reshape(image_rows * cell_count, bin_count), bin_factor, p...  43.8 us
    psum x1, waiting for transfers between devices, body(): gram_bin = lax.psum(bin_local, 'bin')  24.7 us
    all_gather x1, waiting for transfers between devices, body(): lax.all_gather(cell_factor, 'cell', axis=0, tiled=True)[None, :, :]  20.2 us
    another operation x3, other arithmetic, body(): chol_lower = jnp.linalg.cholesky(gram)  12.4 us
    another operation x2, other arithmetic, body(): solved = jax.scipy.linalg.cho_solve((chol_lower, True), totals.T).T  10.5 us
    psum x1, blocking collectives, body(): totals = lax.psum(mttkrp, 'bin')  4.95 us
  transfers between devices with their start and end apart: 3, of which 3 were waited for; matrix products, arithmetic and copies ran while one was open for 11% of the time, Pallas kernels for 0%

commit v1 on v0

--- a/solution.py
+++ b/solution.py
@@ -2,6 +2,27 @@
 import jax.numpy as jnp
 from jax import lax
 from jax.sharding import PartitionSpec as P
+
+
+def gather_around(shard, axis, dim):
+    peers, place, rows = (lax.axis_size(axis), lax.axis_index(axis), shard.shape[dim])
+    right = [(i, (i + 1) % peers) for i in range(peers)]
+    backward = [(i, (i - 1) % peers) for i in range(peers)]
+    out = jnp.zeros((*shard.shape[:dim], peers * rows, *shard.shape[dim + 1 :]), shard.dtype)
+    out = lax.dynamic_update_slice_in_dim(out, shard, place * rows, axis=dim)
+    from_left = from_right = shard
+    halfway = peers // 2
+    for lap in range(1, halfway + 1):
+        from_left = lax.ppermute(from_left, axis, right)
+        out = lax.dynamic_update_slice_in_dim(
+            out, from_left, (place - lap) % peers * rows, axis=dim
+        )
+        if lap < peers - halfway:
+            from_right = lax.ppermute(from_right, axis, backward)
+            out = lax.dynamic_update_slice_in_dim(
+                out, from_right, (place + lap) % peers * rows, axis=dim
+            )
+    return out
 
 
 def body(tensor, cell_factor, bin_factor):
@@ -14,9 +35,7 @@
     projected = projected.reshape(image_rows, cell_count, rank_cols)
     bin_local = jnp.dot(bin_factor.T, bin_factor, precision=highest)
     gram_bin = lax.psum(bin_local, "bin")
-    mttkrp = jnp.sum(
-        projected * lax.all_gather(cell_factor, "cell", axis=0, tiled=True)[None, :, :], axis=1
-    )
+    mttkrp = jnp.sum(projected * gather_around(cell_factor, "cell", 0)[None, :, :], axis=1)
     cell_local = jnp.dot(cell_factor.T, cell_factor, precision=highest)
     gram_cell = lax.psum(cell_local, "cell")
     gram = gram_cell * gram_bin

time: 224 us -> 254 us (1.13)
  starting transfers between devices: 0.09 us -> 32.3 us
  waiting for transfers between devices: 133 us -> 130 us
    ppermute x0 -> x15, starting transfers between devices: none -> 32.2 us  [the longest x7 31.7 us: gather_around(): from_right = lax.ppermute(from_right, axis, backward)]
    ppermute x0 -> x15, waiting for transfers between devices: none -> 23.1 us  [the longest x8 23.1 us: gather_around(): from_left = lax.ppermute(from_left, axis, right)]
    all_gather x1 -> x0, waiting for transfers between devices: 20.2 us -> none  [body(): lax.all_gather(cell_factor, 'cell', axis=0, tiled=True)[None, :, :]]
    psum x1, waiting for transfers between devices: 87.4 us -> 82.2 us  [body(): gram_cell = lax.psum(cell_local, 'cell')]
  transfers between devices with their start and end apart: 3 -> 17, of which waited for: 3 -> 9; matrix products, arithmetic and copies ran while one was open for 11% -> 11% of each run, Pallas kernels for 0% -> 0%
where the time goes in v1:
time: 254 us; the launch traced here: 253 us
  waiting for transfers between devices  130 us (51%)
  matrix products  47.2 us (19%)
  starting transfers between devices  32.3 us (13%)
  other arithmetic  23.7 us (9%)
  between operations  13.9 us (5%)
  blocking collectives  4.95 us (2%)
    psum x1, waiting for transfers between devices, body(): gram_cell = lax.psum(cell_local, 'cell')  82.2 us
    dot_general x1, matrix products, body(): jnp.dot(tensor.reshape(image_rows * cell_count, bin_count), bin_factor, p...  43.5 us
    ppermute x7, starting transfers between devices, gather_around(): from_right = lax.ppermute(from_right, axis, backward)  31.7 us
    psum x1, waiting for transfers between devices, body(): gram_bin = lax.psum(bin_local, 'bin')  24.7 us
    ppermute x8, waiting for transfers between devices, gather_around(): from_left = lax.ppermute(from_left, axis, right)  23.1 us
    another operation x3, other arithmetic, body(): chol_lower = jnp.linalg.cholesky(gram)  12.4 us
    another operation x2, other arithmetic, body(): solved = jax.scipy.linalg.cho_solve((chol_lower, True), totals.T).T  10.5 us
  transfers between devices with their start and end apart: 17, of which 9 were waited for; matrix products, arithmetic and copies ran while one was open for 11% of the time, Pallas kernels for 0%

profile of v1, /device:TPU:0, one launch (start us, length us, event | category | flops | bytes accessed | tf_op | source)
XLA Modules:
  0.0 253.3 jit_solution(5246017661414581719)
XLA Ops:
  6.5 0.0 copy-start
  6.5 0.0 copy-start.1
  6.5 0.0 all-reduce.3.cloned.1.call-start
  6.5 0.5 collective-permute-start
  7.0 5.1 %collective-permute-start.1 = (f32[256,128]{1,0:T(8,128)}, f32[256,128]{1,0:T(8,128)S(1)}, u32[]{:S(2)}, u32[]{:S(2)}) collective-permute-start(f32[256,128]{1,0:T(8,128)} %param.4), channel_id=1, source_target_pairs={{0,30},{2,0},{4,2},{6,4},{8,6},{10,8},{12,10},{14,12},{16,14},{18,... | collective-permute-start | bytes 393224 | tf_op jit(solution)/shard_map/ppermute | solution.py:21
  12.0 2.0 fusion.10
  14.0 0.0 all-reduce.3.cloned.1.call-update
  14.1 0.0 all-reduce.5.cloned.1.call-start
  14.1 0.0 copy-done
  14.1 1.2 fusion.11
  15.3 0.0 all-reduce.5.cloned.1.call-update
  15.7 0.1 mul.65
  15.8 0.0 copy-done.1
  15.8 82.2 %all-reduce.3.cloned.1.call-done = f32[128,128]{0,1:T(8,128)} async-done(((f32[128,128]{0,1:T(8,128)}), f32[128,128]{0,1:T(8,128)}) %all-reduce.3.cloned.1.call-update) | async-done | bytes 65552 | tf_op jit(solution)/shard_map/psum | solution.py:40
  98.0 24.7 %all-reduce.5.cloned.1.call-done = f32[128,128]{0,1:T(8,128)} async-done(((f32[128,128]{0,1:T(8,128)}), f32[128,128]{0,1:T(8,128)}) %all-reduce.5.cloned.1.call-update) | async-done | bytes 65552 | tf_op jit(solution)/shard_map/psum | solution.py:37
  122.8 0.9 mul.64
  123.6 0.1 copy.9
  123.8 11.7 %cholesky.16 = f32[128,128]{1,0:T(8,128)S(1)} custom-call(f32[128,128]{1,0:T(8,128)S(1)} %fusion.9), custom_call_target="Cholesky" | custom-call | tf_op jit(solution)/shard_map/jit(cholesky)/cholesky | solution.py:42
  135.5 0.6 compare_reduce_fusion
  136.2 0.7 fusion.4
  136.8 9.8 %custom-call.10 = f32[1,128,128]{1,2,0:T(8,128)S(1)} custom-call(f32[1,128,128]{2,1,0:T(8,128)S(1)} %fusion.4), custom_call_target="InvertDiagBlocksLowerTriangular" | custom-call | tf_op jit(solution)/shard_map/jit(_cho_solve)/triangular_solve | solution.py:44
  146.6 0.0 collective-permute-done
  146.6 0.1 collective-permute-start.2
  146.7 0.0 collective-permute-done.1
  146.7 4.4 %collective-permute-start.3 = (f32[256,128]{1,0:T(8,128)S(1)}, f32[256,128]{1,0:T(8,128)S(1)}, u32[]{:S(2)}, u32[]{:S(2)}) collective-permute-start(f32[256,128]{1,0:T(8,128)S(1)} %collective-permute-done.1), channel_id=1, source_target_pairs={{0,30},{2,0},{4,2},{6,4},{8,6},{10,8},{12,10},{14,12},{16,14},{18,... | collective-permute-start | bytes 393224 | tf_op jit(solution)/shard_map/ppermute | solution.py:21
  151.2 2.7 %collective-permute-done.2 = f32[256,128]{1,0:T(8,128)S(1)} collective-permute-done((f32[256,128]{1,0:T(8,128)S(1)}, f32[256,128]{1,0:T(8,128)S(1)}, u32[]{:S(2)}, u32[]{:S(2)}) %collective-permute-start.2) | collective-permute-done | bytes 131104 | tf_op jit(solution)/shard_map/ppermute | solution.py:16
  153.9 0.0 collective-permute-start.4
  153.9 0.0 collective-permute-done.3
  153.9 4.4 %collective-permute-start.5 = (f32[256,128]{1,0:T(8,128)S(1)}, f32[256,128]{1,0:T(8,128)S(1)}, u32[]{:S(2)}, u32[]{:S(2)}) collective-permute-start(f32[256,128]{1,0:T(8,128)S(1)} %collective-permute-done.3), channel_id=1, source_target_pairs={{0,30},{2,0},{4,2},{6,4},{8,6},{10,8},{12,10},{14,12},{16,14},{18,... | collective-permute-start | bytes 393224 | tf_op jit(solution)/shard_map/ppermute | solution.py:21
  158.4 2.6 %collective-permute-done.4 = f32[256,128]{1,0:T(8,128)S(1)} collective-permute-done((f32[256,128]{1,0:T(8,128)S(1)}, f32[256,128]{1,0:T(8,128)S(1)}, u32[]{:S(2)}, u32[]{:S(2)}) %collective-permute-start.4) | collective-permute-done | bytes 131104 | tf_op jit(solution)/shard_map/ppermute | solution.py:16
  161.0 0.0 collective-permute-start.6
  161.0 0.0 collective-permute-done.5
  161.0 4.4 %collective-permute-start.7 = (f32[256,128]{1,0:T(8,128)S(1)}, f32[256,128]{1,0:T(8,128)S(1)}, u32[]{:S(2)}, u32[]{:S(2)}) collective-permute-start(f32[256,128]{1,0:T(8,128)S(1)} %collective-permute-done.5), channel_id=1, source_target_pairs={{0,30},{2,0},{4,2},{6,4},{8,6},{10,8},{12,10},{14,12},{16,14},{18,... | collective-permute-start | bytes 393224 | tf_op jit(solution)/shard_map/ppermute | solution.py:21
  165.5 2.7 %collective-permute-done.6 = f32[256,128]{1,0:T(8,128)S(1)} collective-permute-done((f32[256,128]{1,0:T(8,128)S(1)}, f32[256,128]{1,0:T(8,128)S(1)}, u32[]{:S(2)}, u32[]{:S(2)}) %collective-permute-start.6) | collective-permute-done | bytes 131104 | tf_op jit(solution)/shard_map/ppermute | solution.py:16
  168.2 0.0 collective-permute-start.8
  168.2 0.0 collective-permute-done.7
  168.2 4.4 %collective-permute-start.9 = (f32[256,128]{1,0:T(8,128)S(1)}, f32[256,128]{1,0:T(8,128)S(1)}, u32[]{:S(2)}, u32[]{:S(2)}) collective-permute-start(f32[256,128]{1,0:T(8,128)S(1)} %collective-permute-done.7), channel_id=1, source_target_pairs={{0,30},{2,0},{4,2},{6,4},{8,6},{10,8},{12,10},{14,12},{16,14},{18,... | collective-permute-start | bytes 393224 | tf_op jit(solution)/shard_map/ppermute | solution.py:21
  172.7 2.7 %collective-permute-done.8 = f32[256,128]{1,0:T(8,128)S(1)} collective-permute-done((f32[256,128]{1,0:T(8,128)S(1)}, f32[256,128]{1,0:T(8,128)S(1)}, u32[]{:S(2)}, u32[]{:S(2)}) %collective-permute-start.8) | collective-permute-done | bytes 131104 | tf_op jit(solution)/shard_map/ppermute | solution.py:16
  175.4 0.0 collective-permute-start.10
  175.4 0.0 collective-permute-done.9
  175.4 4.4 %collective-permute-start.11 = (f32[256,128]{1,0:T(8,128)S(1)}, f32[256,128]{1,0:T(8,128)S(1)}, u32[]{:S(2)}, u32[]{:S(2)}) collective-permute-start(f32[256,128]{1,0:T(8,128)S(1)} %collective-permute-done.9), channel_id=1, source_target_pairs={{0,30},{2,0},{4,2},{6,4},{8,6},{10,8},{12,10},{14,12},{16,14},{18,... | collective-permute-start | bytes 393224 | tf_op jit(solution)/shard_map/ppermute | solution.py:21
  179.9 2.7 %collective-permute-done.10 = f32[256,128]{1,0:T(8,128)S(1)} collective-permute-done((f32[256,128]{1,0:T(8,128)S(1)}, f32[256,128]{1,0:T(8,128)S(1)}, u32[]{:S(2)}, u32[]{:S(2)}) %collective-permute-start.10) | collective-permute-done | bytes 131104 | tf_op jit(solution)/shard_map/ppermute | solution.py:16
  182.6 0.0 collective-permute-start.12
  182.6 0.0 collective-permute-done.11
  182.6 4.4 %collective-permute-start.13 = (f32[256,128]{1,0:T(8,128)S(1)}, f32[256,128]{1,0:T(8,128)S(1)}, u32[]{:S(2)}, u32[]{:S(2)}) collective-permute-start(f32[256,128]{1,0:T(8,128)S(1)} %collective-permute-done.11), channel_id=1, source_target_pairs={{0,30},{2,0},{4,2},{6,4},{8,6},{10,8},{12,10},{14,12},{16,14},{18,... | collective-permute-start | bytes 393224 | tf_op jit(solution)/shard_map/ppermute | solution.py:21
  187.1 2.6 %collective-permute-done.12 = f32[256,128]{1,0:T(8,128)S(1)} collective-permute-done((f32[256,128]{1,0:T(8,128)S(1)}, f32[256,128]{1,0:T(8,128)S(1)}, u32[]{:S(2)}, u32[]{:S(2)}) %collective-permute-start.12) | collective-permute-done | bytes 131104 | tf_op jit(solution)/shard_map/ppermute | solution.py:16
  189.7 0.0 collective-permute-start.14
  189.7 0.0 collective-permute-done.13
  189.7 7.0 %collective-permute-done.14 = f32[256,128]{1,0:T(8,128)S(1)} collective-permute-done((f32[256,128]{1,0:T(8,128)S(1)}, f32[256,128]{1,0:T(8,128)S(1)}, u32[]{:S(2)}, u32[]{:S(2)}) %collective-permute-start.14) | collective-permute-done | bytes 131104 | tf_op jit(solution)/shard_map/ppermute | solution.py:16
  196.8 43.5 %multiply_reduce_fusion = f32[6,128]{1,0:T(8,128)S(1)} fusion(f32[4096,128]{1,0:T(8,128)S(1)} %constant_dynamic-update-slice_fusion, f32[6,4096,512]{2,1,0:T(8,128)} %param.3, f32[512,128]{1,0:T(8,128)S(1)} %copy-done), kind=kOutput, calls=%fused_computation | convolution fusion | flops 19333644288 | bytes 52694016 | tf_op jit(solution)/shard_map/dot_general | solution.py:32
  240.3 4.9 %psum.23 = f32[6,128]{1,0:T(8,128)S(1)} all-reduce(f32[6,128]{1,0:T(8,128)S(1)} %multiply_reduce_fusion), channel_id=1, replica_groups=mesh['cell'=16,'bin'=2] {'bin'}, use_global_device_ids=true, to_apply=%region_5.6 | all-reduce | flops 768 | bytes 6144 | tf_op jit(solution)/shard_map/psum | solution.py:43
  245.2 0.3 fusion.7
  245.5 0.2 fusion.5
  245.7 0.7 constant_dynamic-slice_fusion
  (18 shorter events, 0.3 us)
Async XLA Ops:
  6.5 7.6 %copy-start = (f32[512,128]{1,0:T(8,128)S(1)}, f32[512,128]{1,0:T(8,128)}, u32[]{:S(2)}) copy-start(f32[512,128]{1,0:T(8,128)} %param.5) | copy-start | bytes 786436
  6.5 9.3 %copy-start.1 = (f32[256,128]{1,0:T(8,128)S(1)}, f32[256,128]{1,0:T(8,128)}, u32[]{:S(2)}) copy-start(f32[256,128]{1,0:T(8,128)} %param.4) | copy-start | bytes 393220
  6.5 91.5 %all-reduce.3.cloned.1.call-start = ((), (), s32[]{:S(2)}) async-start(), calls=%async_computation | async-start | bytes 131072 | tf_op jit(solution)/shard_map/psum | solution.py:40
  6.5 140.1 %collective-permute-start = (f32[256,128]{1,0:T(8,128)}, f32[256,128]{1,0:T(8,128)S(1)}, u32[]{:S(2)}, u32[]{:S(2)}) collective-permute-start(f32[256,128]{1,0:T(8,128)} %param.4), channel_id=1, source_target_pairs={{0,2},{2,4},{4,6},{6,8},{8,10},{10,12},{12,14},{14,16},{16,18},{18... | collective-permute-start | bytes 393224 | tf_op jit(solution)/shard_map/ppermute | solution.py:16
  7.0 139.7 %collective-permute-start.1 = (f32[256,128]{1,0:T(8,128)}, f32[256,128]{1,0:T(8,128)S(1)}, u32[]{:S(2)}, u32[]{:S(2)}) collective-permute-start(f32[256,128]{1,0:T(8,128)} %param.4), channel_id=1, source_target_pairs={{0,30},{2,0},{4,2},{6,4},{8,6},{10,8},{12,10},{14,12},{16,14},{18,... | collective-permute-start | bytes 393224 | tf_op jit(solution)/shard_map/ppermute | solution.py:21
  14.1 108.7 %all-reduce.5.cloned.1.call-start = ((), (), s32[]{:S(2)}) async-start(), calls=%async_computation.1 | async-start | bytes 131072 | tf_op jit(solution)/shard_map/psum | solution.py:37
  146.6 7.2 %collective-permute-start.2 = (f32[256,128]{1,0:T(8,128)S(1)}, f32[256,128]{1,0:T(8,128)S(1)}, u32[]{:S(2)}, u32[]{:S(2)}) collective-permute-start(f32[256,128]{1,0:T(8,128)S(1)} %collective-permute-done), channel_id=1, source_target_pairs={{0,2},{2,4},{4,6},{6,8},{8,10},{10,12},{12,14},{14,16},{16,18},{18... | collective-permute-start | bytes 393224 | tf_op jit(solution)/shard_map/ppermute | solution.py:16
  146.7 7.2 %collective-permute-start.3 = (f32[256,128]{1,0:T(8,128)S(1)}, f32[256,128]{1,0:T(8,128)S(1)}, u32[]{:S(2)}, u32[]{:S(2)}) collective-permute-start(f32[256,128]{1,0:T(8,128)S(1)} %collective-permute-done.1), channel_id=1, source_target_pairs={{0,30},{2,0},{4,2},{6,4},{8,6},{10,8},{12,10},{14,12},{16,14},{18,... | collective-permute-start | bytes 393224 | tf_op jit(solution)/shard_map/ppermute | solution.py:21
  153.9 7.1 %collective-permute-start.4 = (f32[256,128]{1,0:T(8,128)S(1)}, f32[256,128]{1,0:T(8,128)S(1)}, u32[]{:S(2)}, u32[]{:S(2)}) collective-permute-start(f32[256,128]{1,0:T(8,128)S(1)} %collective-permute-done.2), channel_id=1, source_target_pairs={{0,2},{2,4},{4,6},{6,8},{8,10},{10,12},{12,14},{14,16},{16,18},{18... | collective-permute-start | bytes 393224 | tf_op jit(solution)/shard_map/ppermute | solution.py:16
  153.9 7.1 %collective-permute-start.5 = (f32[256,128]{1,0:T(8,128)S(1)}, f32[256,128]{1,0:T(8,128)S(1)}, u32[]{:S(2)}, u32[]{:S(2)}) collective-permute-start(f32[256,128]{1,0:T(8,128)S(1)} %collective-permute-done.3), channel_id=1, source_target_pairs={{0,30},{2,0},{4,2},{6,4},{8,6},{10,8},{12,10},{14,12},{16,14},{18,... | collective-permute-start | bytes 393224 | tf_op jit(solution)/shard_map/ppermute | solution.py:21
  161.0 7.2 %collective-permute-start.6 = (f32[256,128]{1,0:T(8,128)S(1)}, f32[256,128]{1,0:T(8,128)S(1)}, u32[]{:S(2)}, u32[]{:S(2)}) collective-permute-start(f32[256,128]{1,0:T(8,128)S(1)} %collective-permute-done.4), channel_id=1, source_target_pairs={{0,2},{2,4},{4,6},{6,8},{8,10},{10,12},{12,14},{14,16},{16,18},{18... | collective-permute-start | bytes 393224 | tf_op jit(solution)/shard_map/ppermute | solution.py:16
  161.0 7.2 %collective-permute-start.7 = (f32[256,128]{1,0:T(8,128)S(1)}, f32[256,128]{1,0:T(8,128)S(1)}, u32[]{:S(2)}, u32[]{:S(2)}) collective-permute-start(f32[256,128]{1,0:T(8,128)S(1)} %collective-permute-done.5), channel_id=1, source_target_pairs={{0,30},{2,0},{4,2},{6,4},{8,6},{10,8},{12,10},{14,12},{16,14},{18,... | collective-permute-start | bytes 393224 | tf_op jit(solution)/shard_map/ppermute | solution.py:21
  168.2 7.2 %collective-permute-start.8 = (f32[256,128]{1,0:T(8,128)S(1)}, f32[256,128]{1,0:T(8,128)S(1)}, u32[]{:S(2)}, u32[]{:S(2)}) collective-permute-start(f32[256,128]{1,0:T(8,128)S(1)} %collective-permute-done.6), channel_id=1, source_target_pairs={{0,2},{2,4},{4,6},{6,8},{8,10},{10,12},{12,14},{14,16},{16,18},{18... | collective-permute-start | bytes 393224 | tf_op jit(solution)/shard_map/ppermute | solution.py:16
  168.2 7.2 %collective-permute-start.9 = (f32[256,128]{1,0:T(8,128)S(1)}, f32[256,128]{1,0:T(8,128)S(1)}, u32[]{:S(2)}, u32[]{:S(2)}) collective-permute-start(f32[256,128]{1,0:T(8,128)S(1)} %collective-permute-done.7), channel_id=1, source_target_pairs={{0,30},{2,0},{4,2},{6,4},{8,6},{10,8},{12,10},{14,12},{16,14},{18,... | collective-permute-start | bytes 393224 | tf_op jit(solution)/shard_map/ppermute | solution.py:21
  175.4 7.2 %collective-permute-start.10 = (f32[256,128]{1,0:T(8,128)S(1)}, f32[256,128]{1,0:T(8,128)S(1)}, u32[]{:S(2)}, u32[]{:S(2)}) collective-permute-start(f32[256,128]{1,0:T(8,128)S(1)} %collective-permute-done.8), channel_id=1, source_target_pairs={{0,2},{2,4},{4,6},{6,8},{8,10},{10,12},{12,14},{14,16},{16,18},{18... | collective-permute-start | bytes 393224 | tf_op jit(solution)/shard_map/ppermute | solution.py:16
  175.4 7.2 %collective-permute-start.11 = (f32[256,128]{1,0:T(8,128)S(1)}, f32[256,128]{1,0:T(8,128)S(1)}, u32[]{:S(2)}, u32[]{:S(2)}) collective-permute-start(f32[256,128]{1,0:T(8,128)S(1)} %collective-permute-done.9), channel_id=1, source_target_pairs={{0,30},{2,0},{4,2},{6,4},{8,6},{10,8},{12,10},{14,12},{16,14},{18,... | collective-permute-start | bytes 393224 | tf_op jit(solution)/shard_map/ppermute | solution.py:21
  182.6 7.1 %collective-permute-start.12 = (f32[256,128]{1,0:T(8,128)S(1)}, f32[256,128]{1,0:T(8,128)S(1)}, u32[]{:S(2)}, u32[]{:S(2)}) collective-permute-start(f32[256,128]{1,0:T(8,128)S(1)} %collective-permute-done.10), channel_id=1, source_target_pairs={{0,2},{2,4},{4,6},{6,8},{8,10},{10,12},{12,14},{14,16},{16,18},{18... | collective-permute-start | bytes 393224 | tf_op jit(solution)/shard_map/ppermute | solution.py:16
  182.6 7.1 %collective-permute-start.13 = (f32[256,128]{1,0:T(8,128)S(1)}, f32[256,128]{1,0:T(8,128)S(1)}, u32[]{:S(2)}, u32[]{:S(2)}) collective-permute-start(f32[256,128]{1,0:T(8,128)S(1)} %collective-permute-done.11), channel_id=1, source_target_pairs={{0,30},{2,0},{4,2},{6,4},{8,6},{10,8},{12,10},{14,12},{16,14},{18,... | collective-permute-start | bytes 393224 | tf_op jit(solution)/shard_map/ppermute | solution.py:21
  189.7 7.1 %collective-permute-start.14 = (f32[256,128]{1,0:T(8,128)S(1)}, f32[256,128]{1,0:T(8,128)S(1)}, u32[]{:S(2)}, u32[]{:S(2)}) collective-permute-start(f32[256,128]{1,0:T(8,128)S(1)} %collective-permute-done.12), channel_id=1, source_target_pairs={{0,2},{2,4},{4,6},{6,8},{8,10},{10,12},{12,14},{14,16},{16,18},{18... | collective-permute-start | bytes 393224 | tf_op jit(solution)/shard_map/ppermute | solution.py:16
Sparse Core Ops, SparseCore 0:
  14.2 83.8 all-reduce.2
  100.4 22.3 all-reduce.4
